TPU v7x, 512 devices: a whole 4x4x16 slice. The times are simulated.
512 devices in a mesh: dp: 16 (over z), row: 4 (over y), col: 8 (over x, core).
Axes of the slice: x: 4, y: 4, z: 16, core: 2. Of those that a mesh axis runs over, the one named last changes fastest.
Arguments:
- layer_input: bfloat16 [3072, 4096], P(('dp', 'col'), 'row'), may hold values from -6 to 6
- hidden_grad: bfloat16 [3072, 14336], P(('dp', 'row'), 'col'), may hold values from -6 to 6
- gate_slots: bfloat16 [4, 8, 48, 128, 128], P('row', 'col', 'dp'), may hold values from -0.125 to 0.125
- up_slots: bfloat16 [4, 8, 48, 128, 128], P('row', 'col', 'dp'), may hold values from -0.125 to 0.125
- block_mask: int32 [32, 112], replicated, may hold values from 0 to 1, as said below
Outputs:
- input_grad: bfloat16 [3072, 4096], P(('dp', 'col'), 'row')
- gate_slot_grad: float32 [4, 8, 48, 128, 128], P('row', 'col', 'dp')
- up_slot_grad: float32 [4, 8, 48, 128, 128], P('row', 'col', 'dp')
Inputs may be any that keep to these rules, and one draw needn't show every extreme that they name: `block_mask`: every tile of 8 x 14 blocks keeps between 24 and 48 blocks; some tile keeps exactly 48, which tile depends on the draw.
All inputs are finite; a program needn't handle non-finite values.
Results may differ from a plain program's by a relative error of at most 0.022.
Values may be sent and summed in bfloat16 or wider, within the bound.
No kernel may reach another device: no remote copies, remote signals or barrier semaphores. Data moves between devices by JAX's collectives and lax.ppermute only.
A program may use at most 64 MiB of HBM per device.

v0:
```python
import jax
import jax.numpy as jnp
from jax import lax
from jax.sharding import PartitionSpec as P


def slot_maps(block_mask, tile_rows, tile_cols, capacity):
    row_first = lax.axis_index("row") * tile_rows
    col_first = lax.axis_index("col") * tile_cols
    tile_mask = lax.dynamic_slice(block_mask, (row_first, col_first), (tile_rows, tile_cols))
    flat_mask = tile_mask.reshape(tile_rows * tile_cols)
    position = jnp.cumsum(flat_mask) - 1
    slot_ids = jnp.arange(capacity, dtype=jnp.int32)
    chosen = ((flat_mask[:, None] > 0) & (position[:, None] == slot_ids[None, :])).astype(jnp.int32)
    block_ids = jnp.arange(tile_rows * tile_cols, dtype=jnp.int32)
    slot_block = jnp.sum(chosen * block_ids[:, None], axis=0)
    live_slots = jnp.sum(chosen, axis=0).astype(jnp.float32)
    slot_row = slot_block // tile_cols
    slot_col = slot_block % tile_cols
    col_table = (slot_col[:, None] == jnp.arange(tile_cols, dtype=jnp.int32)[None, :]).astype(
        jnp.float32
    ) * live_slots[:, None]
    row_table = (slot_row[:, None] == jnp.arange(tile_rows, dtype=jnp.int32)[None, :]).astype(
        jnp.float32
    ) * live_slots[:, None]
    return (slot_row, slot_col, live_slots, col_table, row_table)


def slot_products(picked, pair_weights, col_table):
    per_slot = jnp.einsum("tsk,skn->tsn", picked, pair_weights, preferred_element_type=jnp.float32)
    return jnp.einsum("tsn,sc->tcn", per_slot, col_table, precision=lax.Precision.HIGHEST)


def back_products(grad_picked, pair_weights, row_table):
    per_slot = jnp.einsum(
        "tsn,skn->tsk", grad_picked, pair_weights, preferred_element_type=jnp.float32
    )
    return jnp.einsum("tsk,sr->trk", per_slot, row_table, precision=lax.Precision.HIGHEST)


def on_device(layer_input, hidden_grad, gate_slots, up_slots, block_mask):
    gate_local = gate_slots[0, 0]
    up_local = up_slots[0, 0]
    block_size = gate_local.shape[-1]
    replicas = lax.axis_size("dp")
    capacity = gate_local.shape[0] * replicas
    token_panel = lax.all_gather(layer_input, "col", axis=0, tiled=True)
    grad_panel = lax.all_gather(hidden_grad, "row", axis=0, tiled=True)
    tok_rows = token_panel.shape[0]
    feat_cols = token_panel.shape[1]
    unit_cols = grad_panel.shape[1]
    tile_rows = feat_cols // block_size
    tile_cols = unit_cols // block_size
    slot_row, slot_col, live_slots, col_table, row_table = slot_maps(
        block_mask, tile_rows, tile_cols, capacity
    )
    token_blocks = token_panel.reshape(tok_rows, tile_rows, block_size)
    picked_tokens = jnp.take(token_blocks, slot_row, axis=1)
    gate_all, up_all = (
        lax.all_gather(gate_local, "dp", axis=0, tiled=True),
        lax.all_gather(up_local, "dp", axis=0, tiled=True),
    )
    pair_all = jnp.concatenate([gate_all, up_all], axis=2)
    pair_part = slot_products(picked_tokens, pair_all, col_table)
    gate_part = pair_part[:, :, :block_size].reshape(tok_rows, unit_cols)
    up_part = pair_part[:, :, block_size:].reshape(tok_rows, unit_cols)
    gate_sum, up_sum = (
        lax.psum(gate_part.astype(jnp.bfloat16), "row").astype(jnp.float32),
        lax.psum(up_part.astype(jnp.bfloat16), "row").astype(jnp.float32),
    )
    sigmoid_gate = jax.nn.sigmoid(gate_sum)
    upstream = grad_panel.astype(jnp.float32)
    gate_grad = (upstream * up_sum * sigmoid_gate * (1.0 + gate_sum * (1.0 - sigmoid_gate))).astype(
        jnp.bfloat16
    )
    up_grad = (upstream * gate_sum * sigmoid_gate).astype(jnp.bfloat16)
    grad_pair = jnp.concatenate(
        [
            gate_grad.reshape(tok_rows, tile_cols, block_size),
            up_grad.reshape(tok_rows, tile_cols, block_size),
        ],
        axis=2,
    )
    grad_picked = jnp.take(grad_pair, slot_col, axis=1)
    summed = back_products(grad_picked, pair_all, row_table)
    input_sum = lax.psum_scatter(
        summed.reshape(tok_rows // lax.axis_size("col") * lax.axis_size("col"), feat_cols).astype(
            jnp.bfloat16
        ),
        "col",
        scatter_dimension=0,
        tiled=True,
    )
    pair_term = (
        jnp.einsum("tsk,tsn->skn", picked_tokens, grad_picked, preferred_element_type=jnp.float32)
        * live_slots[:, None, None]
    )
    pair_total = lax.psum_scatter(
        pair_term.astype(jnp.bfloat16), "dp", scatter_dimension=0, tiled=True
    ).astype(jnp.float32)
    gate_out = (pair_total[:, :, :block_size] / replicas)[None, None]
    up_out = (pair_total[:, :, block_size:] / replicas)[None, None]
    return (input_sum, gate_out, up_out)


def solution(mesh):
    return jax.shard_map(
        on_device,
        mesh=mesh,
        in_specs=(
            P(("dp", "col"), "row"),
            P(("dp", "row"), "col"),
            P("row", "col", "dp", None, None),
            P("row", "col", "dp", None, None),
            P(),
        ),
        out_specs=(
            P(("dp", "col"), "row"),
            P("row", "col", "dp", None, None),
            P("row", "col", "dp", None, None),
        ),
        check_vma=False,
    )
```

profile of v0, /device:TPU:8, one launch (start us, length us, event | category | flops | bytes accessed | tf_op | source)
XLA Modules:
  0.0 370.0 jit_solution(6575437389521833175)
XLA Ops:
  7.2 0.0 all-gather.5.cloned.1.call-start
  7.2 0.7 all-gather.5.cloned.1.call-update
  7.9 0.0 all-gather.7.cloned.1.call-start
  7.9 0.7 all-gather.7.cloned.1.call-update
  8.6 0.0 all-reduce.3.cloned.1.call-start
  8.7 0.8 broadcast_compare_fusion
  9.5 0.1 reshape.169
  9.6 0.2 reduce-window.8
  9.7 0.1 gt.16
  9.8 0.1 add_reduce_fusion
  9.9 0.1 convert_reduce_fusion
  10.1 13.5 %all_gather.15 = bf16[192,1024]{1,0:T(8,128)(2,1)S(1)} all-gather(bf16[24,1024]{1,0:T(8,128)(2,1)} %param.5), channel_id=1, replica_groups=mesh['dp'=16,'row'=4,'col'=8] {'col'}, dimensions={0}, use_global_device_ids=true | all-gather | bytes 442368 | tf_op jit(solution)/shard_map/all_gather | solution.py:47
  23.6 0.1 copy_bitcast_fusion.5
  23.7 1.0 gather_fusion
  24.7 0.0 copy-start
  24.7 61.7 %all-gather.5.cloned.1.call-done = bf16[1,1,48,128,128]{4,3,1,0,2:T(8,128)(2,1)} async-done(((bf16[1,1,3,128,128]{4,3,1,0,2:T(8,128)(2,1)}), bf16[1,1,48,128,128]{4,3,1,0,2:T(8,128)(2,1)}) %all-gather.5.cloned.1.call-update) | async-done | bytes 1572880 | tf_op jit(solution)/shard_map/all_gather | solution.py:60
  86.4 71.1 %all-gather.7.cloned.1.call-done = bf16[1,1,48,128,128]{4,3,1,0,2:T(8,128)(2,1)} async-done(((bf16[1,1,3,128,128]{4,3,1,0,2:T(8,128)(2,1)}), bf16[1,1,48,128,128]{4,3,1,0,2:T(8,128)(2,1)}) %all-gather.7.cloned.1.call-update) | async-done | bytes 1572880 | tf_op jit(solution)/shard_map/all_gather | solution.py:61
  157.5 3.3 convolution_bitcast_fusion
  160.8 0.0 copy-done
  160.8 9.9 %fusion.20 = bf16[192,14,256]{2,1,0:T(8,128)(2,1)S(1)} fusion(f32[192,48,256]{2,0,1:T(8,128)S(1)} %convolution_bitcast_fusion, f32[48]{0:T(128)S(1)} %convert_element_type.55, s32[48]{0:T(128)S(1)} %get-tuple-element.8), kind=kOutput, calls=%fused_computation.23 | convolution fusion | flops 397051200 | bytes 10813824 | tf_op jit(solution)/shard_map/tsn,sc->tcn/dot_general | solution.py:31
  170.7 0.3 fusion.60
  171.0 0.0 copy-start.3
  171.0 1.0 copy.56
  172.1 1.1 copy.57
  173.1 0.0 all-reduce.3.cloned.1.call-update
  173.2 0.0 reduce-scatter.5.cloned.1.call-start
  173.2 0.0 copy-done.3
  173.2 13.2 %all_gather.14 = bf16[192,1792]{1,0:T(8,128)(2,1)S(1)} all-gather(bf16[48,1792]{1,0:T(8,128)(2,1)S(1)} %copy-done.3), channel_id=1, replica_groups=mesh['dp'=16,'row'=4,'col'=8] {'row'}, dimensions={0}, use_global_device_ids=true | all-gather | bytes 860160 | tf_op jit(solution)/shard_map/all_gather | solution.py:48
  186.4 46.7 %all-reduce.3.cloned.1.call-done = (bf16[192,1792]{1,0:T(8,128)(2,1)}, bf16[192,1792]{1,0:T(8,128)(2,1)}) async-done(((bf16[192,1792]{1,0:T(8,128)(2,1)}, bf16[192,1792]{1,0:T(8,128)(2,1)}), (bf16[192,1792]{1,0:T(8,128)(2,1)}, bf16[192,1792]{1,0:T(8,128)(2,1)})) %all-reduce.3.cloned.1.call-update) | async-done | bytes 1376272 | tf_op jit(solution)/shard_map/psum | solution.py:68
  233.1 2.1 fusion.36
  235.1 0.2 copy.58
  235.3 0.2 copy.59
  235.5 0.2 pad_maximum_fusion.3
  235.7 3.1 gather_fusion.1
  238.8 6.2 %multiply_convert_fusion = bf16[48,128,256]{2,1,0:T(8,128)(2,1)} fusion(f32[48]{0:T(128)S(1)} %convert_element_type.55, bf16[48,192,256]{2,1,0:T(8,128)(2,1)} %gather_fusion.1, pred[48]{0:T(512)(128)(4,1)S(1)} %get-tuple-element.7, bf16[48,192,128]{2,1,0:T(8,128)(2,1)} %copy-done, pred[48]{0:T(512)(128)(4,1)S(1)} %get-tuple-element.22), kind=kOutput, calls=%fused_computation.4 | convolution fusion | flops 610664448 | bytes 10223904 | tf_op jit(solution)/shard_map/tsk,tsn->skn/dot_general | solution.py:95
  245.1 0.0 copy-start.1
  245.1 0.0 copy-start.2
  245.1 0.0 reduce-scatter.5.cloned.1.call-update
  245.1 0.0 reduce-scatter.3.cloned.1.call-start
  245.1 1.3 copy-done.1
  246.5 0.5 copy-done.2
  246.9 3.3 fusion.10
  250.3 4.9 %fusion.32 = bf16[8,192,128]{2,0,1:T(8,128)(2,1)S(1)} fusion(f32[192,48,128]{2,0,1:T(8,128)S(1)} %fusion.10, f32[48]{0:T(128)S(1)} %convert_element_type.55, s32[48]{0:T(128)S(1)} %get-tuple-element.23), kind=kOutput, calls=%fused_computation.34 | convolution fusion | flops 113443584 | bytes 5112192 | tf_op jit(solution)/shard_map/tsk,sr->trk/dot_general | solution.py:38
  255.2 0.8 copy.60
  256.0 0.0 reduce-scatter.3.cloned.1.call-update
  256.0 67.8 %reduce-scatter.5.cloned.1.call-done = bf16[3,128,256]{2,1,0:T(8,128)(2,1)} async-done(((bf16[48,128,256]{2,1,0:T(8,128)(2,1)}), bf16[3,128,256]{2,1,0:T(8,128)(2,1)}) %reduce-scatter.5.cloned.1.call-update) | async-done | bytes 196624 | tf_op jit(solution)/shard_map/reduce_scatter | solution.py:98
  323.8 1.0 convert_element_type.67
  324.8 0.8 fusion.37
  325.5 38.0 %reduce-scatter.3.cloned.1.call-done = bf16[24,1024]{1,0:T(8,128)(2,1)} async-done(((bf16[192,1024]{1,0:T(8,128)(2,1)}), bf16[24,1024]{1,0:T(8,128)(2,1)}) %reduce-scatter.3.cloned.1.call-update) | async-done | bytes 49168 | tf_op jit(solution)/shard_map/reduce_scatter | solution.py:86
  (4 shorter events, 0.1 us)
Async XLA Ops:
  7.2 79.3 %all-gather.5.cloned.1.call-start = ((), (), s32[]{:S(2)}) async-start(), calls=%async_computation.4 | async-start | bytes 1671168 | tf_op jit(solution)/shard_map/all_gather | solution.py:60
  7.9 149.6 %all-gather.7.cloned.1.call-start = ((), (), s32[]{:S(2)}) async-start(), calls=%async_computation.5 | async-start | bytes 1671168 | tf_op jit(solution)/shard_map/all_gather | solution.py:61
  8.6 224.4 %all-reduce.3.cloned.1.call-start = ((), (), s32[]{:S(2)}) async-start(), calls=%async_computation.6 | async-start | bytes 2752512 | tf_op jit(solution)/shard_map/psum | solution.py:68
  24.7 136.1 %copy-start = (bf16[48,192,128]{2,1,0:T(8,128)(2,1)}, bf16[48,192,128]{2,1,0:T(8,128)(2,1)S(1)}, u32[]{:S(2)}) copy-start(bf16[48,192,128]{2,1,0:T(8,128)(2,1)S(1)} %gather_fusion) | copy-start | bytes 7077892
  171.0 2.2 copy-start.3
  173.2 150.6 %reduce-scatter.5.cloned.1.call-start = ((), (), s32[]{:S(2)}) async-start(), calls=%async_computation.3 | async-start | bytes 3342336 | tf_op jit(solution)/shard_map/reduce_scatter | solution.py:98
  245.1 1.4 copy-start.1
  245.1 1.9 copy-start.2
  245.1 118.4 %reduce-scatter.3.cloned.1.call-start = ((), (), s32[]{:S(2)}) async-start(), calls=%async_computation.2 | async-start | bytes 442368 | tf_op jit(solution)/shard_map/reduce_scatter | solution.py:86
Sparse Core Ops, SparseCore 0:
  10.0 76.3 all-gather.4
  88.5 68.9 all-gather.6
  173.3 59.7 all-reduce.2
  245.2 78.5 reduce-scatter.4
  327.0 36.4 reduce-scatter.2
where the time goes:
time: 370 us
  waiting for transfers between devices  287 us (78%)
  matrix products  27.7 us (7%)
  blocking collectives  26.7 us (7%)
  between operations  13.9 us (4%)
  local copies, waits for them, and re-layouts  9.72 us (3%)
  other arithmetic  5.19 us (1%)
    all_gather x1, waiting for transfers between devices, on_device(): lax.all_gather(up_local, 'dp', axis=0, tiled=True)  71.1 us
    reduce_scatter x1, waiting for transfers between devices, on_device(): lax.psum_scatter(pair_term.astype(jnp.bfloat16), 'dp', scatter_dimension=...  67.8 us
    all_gather x1, waiting for transfers between devices, on_device(): lax.all_gather(gate_local, 'dp', axis=0, tiled=True)  61.7 us
    psum x1, waiting for transfers between devices, on_device(): lax.psum(gate_part.astype(jnp.bfloat16), 'row').astype(jnp.float32)  46.7 us
    reduce_scatter x1, waiting for transfers between devices, on_device(): lax.psum_scatter(summed.reshape(tok_rows // lax.axis_size('col') * lax.ax...  38 us
    all_gather x1, blocking collectives, on_device(): token_panel = lax.all_gather(layer_input, 'col', axis=0, tiled=True)  13.5 us
    all_gather x1, blocking collectives, on_device(): grad_panel = lax.all_gather(hidden_grad, 'row', axis=0, tiled=True)  13.2 us
    dot_general x1, matrix products, slot_products(): jnp.einsum('tsn,sc->tcn', per_slot, col_table, precision=lax.Precision.HI...  9.9 us
  transfers between devices with their start and end apart: 5, of which 5 were waited for; matrix products, arithmetic and copies ran while one was open for 4% of the time, Pallas kernels for 0%

commit v1 on v0

--- a/solution.py
+++ b/solution.py
@@ -44,7 +44,10 @@
     block_size = gate_local.shape[-1]
     replicas = lax.axis_size("dp")
     capacity = gate_local.shape[0] * replicas
-    token_panel = lax.all_gather(layer_input, "col", axis=0, tiled=True)
+    val2 = lax.axis_size("col")
+    even = jnp.stack(val2 * [layer_input])
+    small = lax.all_to_all(even, axis_name="col", split_axis=0, concat_axis=0)
+    token_panel = jnp.concatenate(small, axis=0)
     grad_panel = lax.all_gather(hidden_grad, "row", axis=0, tiled=True)
     tok_rows = token_panel.shape[0]
     feat_cols = token_panel.shape[1]

time: 370 us -> 370 us (level)
  blocking collectives: 26.7 us -> 13.2 us
  waiting for transfers between devices: 287 us -> 294 us
  starting transfers between devices: 0.2 us -> 4.5 us
    all_gather x1 -> x0, blocking collectives: 13.5 us -> none  [on_device(): token_panel = lax.all_gather(layer_input, 'col', axis=0, tiled=True)]
    all_to_all x0 -> x1, waiting for transfers between devices: none -> 7.45 us  [on_device(): small = lax.all_to_all(even, axis_name='col', split_axis=0, concat_axis=0)]
    all_to_all x0 -> x1, starting transfers between devices: none -> 4.3 us  [on_device(): small = lax.all_to_all(even, axis_name='col', split_axis=0, concat_axis=0)]
  transfers between devices with their start and end apart: 5 -> 6, of which waited for: 5 -> 6; matrix products, arithmetic and copies ran while one was open for 4% -> 4% of each run, Pallas kernels for 0% -> 0%
where the time goes in v1:
time: 370 us
  waiting for transfers between devices  294 us (79%)
  matrix products  27.7 us (7%)
  between operations  13.9 us (4%)
  blocking collectives  13.2 us (4%)
  local copies, waits for them, and re-layouts  11.3 us (3%)
  other arithmetic  5.19 us (1%)
  starting transfers between devices  4.5 us (1%)
    all_gather x1, waiting for transfers between devices, on_device(): lax.all_gather(up_local, 'dp', axis=0, tiled=True)  71.1 us
    reduce_scatter x1, waiting for transfers between devices, on_device(): lax.psum_scatter(pair_term.astype(jnp.bfloat16), 'dp', scatter_dimension=...  67.9 us
    all_gather x1, waiting for transfers between devices, on_device(): lax.all_gather(gate_local, 'dp', axis=0, tiled=True)  61.8 us
    psum x1, waiting for transfers between devices, on_device(): lax.psum(gate_part.astype(jnp.bfloat16), 'row').astype(jnp.float32)  46.6 us
    reduce_scatter x1, waiting for transfers between devices, on_device(): lax.psum_scatter(summed.reshape(tok_rows // lax.axis_size('col') * lax.ax...  37.9 us
    all_gather x1, blocking collectives, on_device(): grad_panel = lax.all_gather(hidden_grad, 'row', axis=0, tiled=True)  13.2 us
    dot_general x1, matrix products, slot_products(): jnp.einsum('tsn,sc->tcn', per_slot, col_table, precision=lax.Precision.HI...  9.9 us
    all_to_all x1, waiting for transfers between devices, on_device(): small = lax.all_to_all(even, axis_name='col', split_axis=0, concat_axis=0)  7.45 us
  transfers between devices with their start and end apart: 6, of which 6 were waited for; matrix products, arithmetic and copies ran while one was open for 4% of the time, Pallas kernels for 0%

profile of v1, /device:TPU:8, one launch (start us, length us, event | category | flops | bytes accessed | tf_op | source)
XLA Modules:
  0.0 370.1 jit_solution(15470832604757055481)
XLA Ops:
  7.2 0.0 all-gather.5.cloned.1.call-start
  7.2 0.7 all-gather.5.cloned.1.call-update
  7.9 0.0 all-gather.7.cloned.1.call-start
  7.9 0.7 all-gather.7.cloned.1.call-update
  8.6 1.6 stack.2
  10.2 4.3 %all-to-all-start = ((bf16[8,24,1024]{2,1,0:T(8,128)(2,1)}), bf16[8,24,1024]{2,1,0:T(8,128)(2,1)S(1)}, u32[]{:S(2)}, u32[]{:S(2)}) async-start(bf16[8,24,1024]{2,1,0:T(8,128)(2,1)} %stack.2), calls=%async_computation | async-start | bytes 786432 | tf_op jit(solution)/shard_map/all_to_all | solution.py:49
  14.5 0.0 all-reduce.3.cloned.1.call-start
  14.6 0.8 broadcast_compare_fusion
  15.4 0.1 reshape.167
  15.4 0.2 reduce-window.8
  15.6 0.1 gt.16
  15.7 0.1 add_reduce_fusion
  15.8 0.1 convert_reduce_fusion
  16.0 7.4 %all-to-all-done = bf16[8,24,1024]{2,1,0:T(8,128)(2,1)S(1)} async-done(((bf16[8,24,1024]{2,1,0:T(8,128)(2,1)}), bf16[8,24,1024]{2,1,0:T(8,128)(2,1)S(1)}, u32[]{:S(2)}, u32[]{:S(2)}) %all-to-all-start) | async-done | bytes 393248 | tf_op jit(solution)/shard_map/all_to_all | solution.py:49
  23.4 0.1 copy.36
  23.5 0.1 copy.29
  23.6 1.0 gather_fusion
  24.6 0.0 copy-start
  24.6 61.8 %all-gather.5.cloned.1.call-done = bf16[1,1,48,128,128]{4,3,1,0,2:T(8,128)(2,1)} async-done(((bf16[1,1,3,128,128]{4,3,1,0,2:T(8,128)(2,1)}), bf16[1,1,48,128,128]{4,3,1,0,2:T(8,128)(2,1)}) %all-gather.5.cloned.1.call-update) | async-done | bytes 1572880 | tf_op jit(solution)/shard_map/all_gather | solution.py:63
  86.4 71.1 %all-gather.7.cloned.1.call-done = bf16[1,1,48,128,128]{4,3,1,0,2:T(8,128)(2,1)} async-done(((bf16[1,1,3,128,128]{4,3,1,0,2:T(8,128)(2,1)}), bf16[1,1,48,128,128]{4,3,1,0,2:T(8,128)(2,1)}) %all-gather.7.cloned.1.call-update) | async-done | bytes 1572880 | tf_op jit(solution)/shard_map/all_gather | solution.py:64
  157.5 3.3 convolution_bitcast_fusion
  160.8 0.0 copy-done
  160.8 9.9 %fusion.20 = bf16[192,14,256]{2,1,0:T(8,128)(2,1)S(1)} fusion(f32[192,48,256]{2,0,1:T(8,128)S(1)} %convolution_bitcast_fusion, f32[48]{0:T(128)S(1)} %convert_element_type.55, s32[48]{0:T(128)S(1)} %get-tuple-element.8), kind=kOutput, calls=%fused_computation.23 | convolution fusion | flops 397051200 | bytes 10813824 | tf_op jit(solution)/shard_map/tsn,sc->tcn/dot_general | solution.py:31
  170.7 0.3 fusion.60
  171.0 0.0 copy-start.3
  171.0 1.0 copy.55
  172.1 1.0 copy.56
  173.1 0.0 all-reduce.3.cloned.1.call-update
  173.1 0.0 reduce-scatter.5.cloned.1.call-start
  173.2 0.0 copy-done.3
  173.2 13.2 %all_gather.11 = bf16[192,1792]{1,0:T(8,128)(2,1)S(1)} all-gather(bf16[48,1792]{1,0:T(8,128)(2,1)S(1)} %copy-done.3), channel_id=1, replica_groups=mesh['dp'=16,'row'=4,'col'=8] {'row'}, dimensions={0}, use_global_device_ids=true | all-gather | bytes 860160 | tf_op jit(solution)/shard_map/all_gather | solution.py:51
  186.3 46.6 %all-reduce.3.cloned.1.call-done = (bf16[192,1792]{1,0:T(8,128)(2,1)}, bf16[192,1792]{1,0:T(8,128)(2,1)}) async-done(((bf16[192,1792]{1,0:T(8,128)(2,1)}, bf16[192,1792]{1,0:T(8,128)(2,1)}), (bf16[192,1792]{1,0:T(8,128)(2,1)}, bf16[192,1792]{1,0:T(8,128)(2,1)})) %all-reduce.3.cloned.1.call-update) | async-done | bytes 1376272 | tf_op jit(solution)/shard_map/psum | solution.py:71
  233.0 2.1 fusion.36
  235.1 0.2 copy.57
  235.2 0.2 copy.58
  235.4 0.2 pad_maximum_fusion.3
  235.6 3.1 gather_fusion.1
  238.8 6.3 %multiply_convert_fusion = bf16[48,128,256]{2,1,0:T(8,128)(2,1)} fusion(f32[48]{0:T(128)S(1)} %convert_element_type.55, bf16[48,192,256]{2,1,0:T(8,128)(2,1)} %gather_fusion.1, pred[48]{0:T(512)(128)(4,1)S(1)} %get-tuple-element.7, bf16[48,192,128]{2,1,0:T(8,128)(2,1)} %copy-done, pred[48]{0:T(512)(128)(4,1)S(1)} %get-tuple-element.22), kind=kOutput, calls=%fused_computation.4 | convolution fusion | flops 610664448 | bytes 10223904 | tf_op jit(solution)/shard_map/tsk,tsn->skn/dot_general | solution.py:98
  245.0 0.0 copy-start.1
  245.0 0.0 copy-start.2
  245.0 0.0 reduce-scatter.5.cloned.1.call-update
  245.0 0.0 reduce-scatter.3.cloned.1.call-start
  245.1 1.3 copy-done.1
  246.4 0.5 copy-done.2
  246.9 3.3 fusion.10
  250.2 4.9 %fusion.32 = bf16[8,192,128]{2,0,1:T(8,128)(2,1)S(1)} fusion(f32[192,48,128]{2,0,1:T(8,128)S(1)} %fusion.10, f32[48]{0:T(128)S(1)} %convert_element_type.55, s32[48]{0:T(128)S(1)} %get-tuple-element.23), kind=kOutput, calls=%fused_computation.34 | convolution fusion | flops 113443584 | bytes 5112192 | tf_op jit(solution)/shard_map/tsk,sr->trk/dot_general | solution.py:38
  255.1 0.8 copy.59
  256.0 0.0 reduce-scatter.3.cloned.1.call-update
  256.0 67.9 %reduce-scatter.5.cloned.1.call-done = bf16[3,128,256]{2,1,0:T(8,128)(2,1)} async-done(((bf16[48,128,256]{2,1,0:T(8,128)(2,1)}), bf16[3,128,256]{2,1,0:T(8,128)(2,1)}) %reduce-scatter.5.cloned.1.call-update) | async-done | bytes 196624 | tf_op jit(solution)/shard_map/reduce_scatter | solution.py:101
  323.9 1.0 convert_element_type.67
  324.9 0.8 fusion.37
  325.6 37.9 %reduce-scatter.3.cloned.1.call-done = bf16[24,1024]{1,0:T(8,128)(2,1)} async-done(((bf16[192,1024]{1,0:T(8,128)(2,1)}), bf16[24,1024]{1,0:T(8,128)(2,1)}) %reduce-scatter.3.cloned.1.call-update) | async-done | bytes 49168 | tf_op jit(solution)/shard_map/reduce_scatter | solution.py:89
  (4 shorter events, 0.1 us)
Async XLA Ops:
  7.2 79.3 %all-gather.5.cloned.1.call-start = ((), (), s32[]{:S(2)}) async-start(), calls=%async_computation.5 | async-start | bytes 1671168 | tf_op jit(solution)/shard_map/all_gather | solution.py:63
  7.9 149.6 %all-gather.7.cloned.1.call-start = ((), (), s32[]{:S(2)}) async-start(), calls=%async_computation.6 | async-start | bytes 1671168 | tf_op jit(solution)/shard_map/all_gather | solution.py:64
  10.2 13.2 %all-to-all-start = ((bf16[8,24,1024]{2,1,0:T(8,128)(2,1)}), bf16[8,24,1024]{2,1,0:T(8,128)(2,1)S(1)}, u32[]{:S(2)}, u32[]{:S(2)}) async-start(bf16[8,24,1024]{2,1,0:T(8,128)(2,1)} %stack.2), calls=%async_computation | async-start | bytes 786432 | tf_op jit(solution)/shard_map/all_to_all | solution.py:49
  14.5 218.5 %all-reduce.3.cloned.1.call-start = ((), (), s32[]{:S(2)}) async-start(), calls=%async_computation.7 | async-start | bytes 2752512 | tf_op jit(solution)/shard_map/psum | solution.py:71
  24.6 136.2 %copy-start = (bf16[48,192,128]{2,1,0:T(8,128)(2,1)}, bf16[48,192,128]{2,1,0:T(8,128)(2,1)S(1)}, u32[]{:S(2)}) copy-start(bf16[48,192,128]{2,1,0:T(8,128)(2,1)S(1)} %gather_fusion) | copy-start | bytes 7077892
  171.0 2.2 copy-start.3
  173.1 150.8 %reduce-scatter.5.cloned.1.call-start = ((), (), s32[]{:S(2)}) async-start(), calls=%async_computation.4 | async-start | bytes 3342336 | tf_op jit(solution)/shard_map/reduce_scatter | solution.py:101
  245.0 1.4 copy-start.1
  245.0 1.9 copy-start.2
  245.0 118.5 %reduce-scatter.3.cloned.1.call-start = ((), (), s32[]{:S(2)}) async-start(), calls=%async_computation.3 | async-start | bytes 442368 | tf_op jit(solution)/shard_map/reduce_scatter | solution.py:89
Sparse Core Ops, SparseCore 0:
  10.0 76.3 all-gather.4
  88.5 68.9 all-gather.6
  173.2 59.6 all-reduce.2
  245.2 78.6 reduce-scatter.4
  327.1 36.3 reduce-scatter.2
